TPU v7x, 32 devices: a whole 2x2x4 slice. The times are simulated.
32 devices in a mesh: groups: 2 (over y), ctx: 4 (over z), sub: 2 (over x), head: 2 (over core).
Axes of the slice: x: 2, y: 2, z: 4, core: 2. Of those that a mesh axis runs over, the one named last changes fastest.
Arguments:
- queries: bfloat16 [32, 10240, 128], P(('sub', 'head'), ('groups', 'ctx')), parts along dimension 1, may hold values from -6 to 6
- keys: bfloat16 [32, 10240, 128], P(('sub', 'head'), ('groups', 'ctx')), parts along dimension 1, may hold values from -6 to 6
- values: bfloat16 [32, 10240, 128], P(('sub', 'head'), ('groups', 'ctx')), parts along dimension 1, may hold values from -90 to 90
- out_grad: bfloat16 [32, 10240, 128], P(('sub', 'head'), ('groups', 'ctx')), parts along dimension 1, may hold values from -6 to 6
- norm_gain: float32 [32, 128], P(('sub', 'head')), may hold values from 0.25 to 1.75
- doc_ids: int32 [40], P(('groups', 'ctx')), parts along dimension 0, may hold values from 0 to 3, never falling along the last dimension, each value on 1 to 10 neighbouring positions
Outputs:
- grad_queries: bfloat16 [32, 10240, 128], P(('sub', 'head'), ('groups', 'ctx')), parts along dimension 1
- grad_keys: bfloat16 [32, 10240, 128], P(('sub', 'head'), ('groups', 'ctx')), parts along dimension 1
- grad_values: bfloat16 [32, 10240, 128], P(('sub', 'head'), ('groups', 'ctx')), parts along dimension 1
There are 2 independent parts, one for each index of `groups`. A program takes and returns all parts, laid end to end along the dimension named above; an argument that names none is the same for every part. Nothing has to cross between parts.
Inputs may be any that keep to these rules, and one draw needn't show every extreme that they name: `doc_ids`: never falls; each of its 4 values labels 1 to 10 consecutive blocks, one value exactly 10.
All inputs are finite; a program needn't handle non-finite values.
Results may differ from a plain program's by a relative error of at most 0.0058.
Values sent between devices are 32-bit elements; how exact they have to be, the bound alone decides.
No kernel may reach another device: no remote copies, remote signals or barrier semaphores. Data moves between devices by JAX's collectives and lax.ppermute only.
A program may use at most 128 MiB of HBM per device.

v0:
```python
import jax
import jax.numpy as jnp
from jax import lax
from jax.sharding import PartitionSpec as P


def segmented_scan(doc, state, axis, reverse):
    peers = lax.axis_size(axis)
    index = lax.axis_index(axis)
    none_doc = jnp.float32(-1.0)

    def shift(value, step):
        if reverse:
            pairs = [(j, j - step) for j in range(step, peers)]
        else:
            pairs = [(j, j + step) for j in range(peers - step)]
        return lax.ppermute(value, axis, pairs)

    def combine(near_doc, near_state, far_doc, far_state):
        joined = (near_doc == far_doc).astype(jnp.float32)
        return (near_doc, near_state + joined * far_state)

    if peers == 1:
        return (none_doc, jnp.zeros_like(state))
    got_doc, got_state = shift((doc, state), 1)
    valid = index >= 1 if not reverse else index <= peers - 2
    ex_doc = jnp.where(valid, got_doc, none_doc)
    ex_state = jnp.where(valid, got_state, 0.0)
    in_doc, in_state = combine(doc, state, ex_doc, ex_state)
    covered = 1
    while covered < peers - 1:
        step = covered + 1
        got_doc, got_state = shift((in_doc, in_state), step)
        valid = index >= step if not reverse else index <= peers - 1 - step
        got_doc = jnp.where(valid, got_doc, none_doc)
        got_state = jnp.where(valid, got_state, 0.0)
        ex_doc, ex_state = combine(ex_doc, ex_state, got_doc, got_state)
        covered = covered + step
        if covered < peers - 1:
            in_doc, in_state = combine(in_doc, in_state, got_doc, got_state)
    return (ex_doc, ex_state)


def on_device(queries, keys, values, out_grad, norm_gain, doc_ids):
    head_count, tok_count, head_width = queries.shape
    block_count = doc_ids.shape[0]
    block_len = tok_count // block_count
    block_shape = (head_count, block_count, block_len, head_width)
    highest_precision = lax.Precision.HIGHEST
    query_blocks = queries.reshape(block_shape)
    key_blocks = keys.reshape(block_shape)
    value_blocks = values.reshape(block_shape)
    row_ids = lax.broadcasted_iota(jnp.int32, (block_len, block_len), 0)
    col_ids = lax.broadcasted_iota(jnp.int32, (block_len, block_len), 1)
    causal = row_ids >= col_ids
    doc_values = doc_ids.astype(jnp.float32)
    block_pos = jnp.arange(block_count, dtype=jnp.int32)
    same_doc = doc_values[:, None] == doc_values[None, :]
    earlier_mask = (same_doc & (block_pos[None, :] < block_pos[:, None])).astype(jnp.float32)
    later_mask = (same_doc & (block_pos[None, :] > block_pos[:, None])).astype(jnp.float32)
    key_value_block = jnp.einsum(
        "hnid,hnie->hnde", key_blocks, value_blocks, preferred_element_type=jnp.float32
    )
    last_match = (doc_values == doc_values[-1]).astype(jnp.float32)
    device_kv = jnp.einsum("c,hcde->hde", last_match, key_value_block, precision=highest_precision)
    prior_doc, prior_state = segmented_scan(doc_values[-1], device_kv, "ctx", False)
    scores = jnp.einsum(
        "hnid,hnjd->hnij", query_blocks, key_blocks, preferred_element_type=jnp.float32
    )
    block_probs = jnp.where(causal, scores, 0.0).astype(jnp.bfloat16)
    intra_part = jnp.einsum(
        "hnij,hnjd->hnid", block_probs, value_blocks, preferred_element_type=jnp.float32
    )
    local_prefix = jnp.einsum(
        "bc,hcde->hbde", earlier_mask, key_value_block, precision=highest_precision
    )
    prior_match = (doc_values == prior_doc).astype(jnp.float32)
    entering = prior_match[None, :, None, None] * prior_state[:, None, :, :]
    preceding_states = (local_prefix + entering).astype(jnp.bfloat16)
    cross_block_part = jnp.einsum(
        "hnid,hnde->hnie", query_blocks, preceding_states, preferred_element_type=jnp.float32
    )
    raw_attn = (intra_part + cross_block_part).reshape(head_count, tok_count, head_width)
    feature_count = head_count * head_width * lax.axis_size(("sub", "head"))
    scaled = norm_gain[:, None, :] * out_grad.astype(jnp.float32)
    local_sums = jnp.stack(
        [jnp.sum(raw_attn * raw_attn, axis=(0, 2)), jnp.sum(scaled * raw_attn, axis=(0, 2))]
    )
    total_sums = lax.psum(local_sums, ("sub", "head"))
    root_mean = jnp.sqrt(total_sums[0] / feature_count + 1e-06)
    inner_mean = total_sums[1] / feature_count
    factor = inner_mean / (root_mean * root_mean)
    d_attn = ((scaled - raw_attn * factor[None, :, None]) / root_mean[None, :, None]).astype(
        jnp.bfloat16
    )
    output_grad_blocks = d_attn.reshape(block_shape)
    query_grad_block = jnp.einsum(
        "hnid,hnie->hnde", query_blocks, output_grad_blocks, preferred_element_type=jnp.float32
    )
    first_match = (doc_values == doc_values[0]).astype(jnp.float32)
    device_qd = jnp.einsum(
        "c,hcde->hde", first_match, query_grad_block, precision=highest_precision
    )
    next_doc, next_state = segmented_scan(doc_values[0], device_qd, "ctx", True)
    grad_scores = jnp.einsum(
        "hnid,hnjd->hnij", output_grad_blocks, value_blocks, preferred_element_type=jnp.float32
    )
    grad_probs = jnp.where(causal, grad_scores, 0.0).astype(jnp.bfloat16)
    query_gradient = jnp.einsum(
        "hnij,hnjd->hnid", grad_probs, key_blocks, preferred_element_type=jnp.float32
    )
    key_gradient = jnp.einsum(
        "hnij,hnid->hnjd", grad_probs, query_blocks, preferred_element_type=jnp.float32
    )
    value_gradient = jnp.einsum(
        "hnij,hnid->hnjd", block_probs, output_grad_blocks, preferred_element_type=jnp.float32
    )
    local_suffix = jnp.einsum(
        "bc,hcde->hbde", later_mask, query_grad_block, precision=highest_precision
    )
    next_match = (doc_values == next_doc).astype(jnp.float32)
    leaving = next_match[None, :, None, None] * next_state[:, None, :, :]
    following_states = (local_suffix + leaving).astype(jnp.bfloat16)
    query_gradient = query_gradient + jnp.einsum(
        "hnie,hnde->hnid", output_grad_blocks, preceding_states, preferred_element_type=jnp.float32
    )
    key_gradient = key_gradient + jnp.einsum(
        "hnie,hnde->hnid", value_blocks, following_states, preferred_element_type=jnp.float32
    )
    value_gradient = value_gradient + jnp.einsum(
        "hnid,hnde->hnie", key_blocks, following_states, preferred_element_type=jnp.float32
    )
    out_shape = (head_count, tok_count, head_width)
    return (
        query_gradient.reshape(out_shape).astype(jnp.bfloat16),
        key_gradient.reshape(out_shape).astype(jnp.bfloat16),
        value_gradient.reshape(out_shape).astype(jnp.bfloat16),
    )


def solution(mesh):
    return jax.shard_map(
        on_device,
        mesh=mesh,
        in_specs=(
            P(("sub", "head"), ("groups", "ctx"), None),
            P(("sub", "head"), ("groups", "ctx"), None),
            P(("sub", "head"), ("groups", "ctx"), None),
            P(("sub", "head"), ("groups", "ctx"), None),
            P(("sub", "head"), None),
            P(("groups", "ctx")),
        ),
        out_specs=(
            P(("sub", "head"), ("groups", "ctx"), None),
            P(("sub", "head"), ("groups", "ctx"), None),
            P(("sub", "head"), ("groups", "ctx"), None),
        ),
        check_vma=False,
    )
```

profile of v0, /device:TPU:0, one launch (start us, length us, event | category | flops | bytes accessed | tf_op | source)
XLA Modules:
  0.0 159.0 jit_solution(8993034932632156992)
XLA Ops:
  2.0 1.3 collective-permute-start.6
  3.3 1.3 collective-permute-start.4
  4.6 7.6 %collective-permute-start.2 = (f32[]{:T(128)}, f32[]{:T(128)}, u32[]{:S(2)}, u32[]{:S(2)}) collective-permute-start(f32[]{:T(128)} %bitcast.7), channel_id=1, source_target_pairs={{0,8},{4,12},{1,9},{5,13},{2,10},{6,14},{3,11},{7,15},{16,24},{20,... | collective-permute-start | bytes 20 | tf_op jit(solution)/shard_map/ppermute | solution.py:17
  12.2 5.0 %collective-permute-start = (f32[]{:T(128)}, f32[]{:T(128)}, u32[]{:S(2)}, u32[]{:S(2)}) collective-permute-start(f32[]{:T(128)} %bitcast.7), channel_id=1, source_target_pairs={{0,4},{4,8},{8,12},{1,5},{5,9},{9,13},{2,6},{6,10},{10,14},{3,7},{... | collective-permute-start | bytes 20 | tf_op jit(solution)/shard_map/ppermute | solution.py:17
  17.2 3.4 %fusion.36 = f32[8,5,128,128]{3,2,1,0:T(8,128)S(1)} fusion(bf16[8,5,256,128]{3,2,1,0:T(8,128)(2,1)} %bitcast.105, bf16[8,5,256,128]{3,2,1,0:T(8,128)(2,1)} %bitcast.109), kind=kOutput, calls=%fused_computation.62 | convolution fusion | flops 335544320 | bytes 7864320 | tf_op jit(solution)/shard_map/hnid,hnie->hnde/dot_general | solution.py:61
  20.6 1.5 copy-done.2
  22.1 4.9 %fusion.6 = f32[1,8,128,128]{3,0,2,1:T(1,128)} fusion(f32[8,5,128,128]{3,2,1,0:T(8,128)S(1)} %fusion.36, f32[]{:T(128)} %bitcast.7, s32[5]{0:T(128)S(1)} %copy-done.16), kind=kOutput, calls=%fused_computation.16 | convolution fusion | flops 7864330 | bytes 3145752 | tf_op jit(solution)/shard_map/c,hcde->hde/dot_general | solution.py:65
  27.0 1.4 collective-permute-start.1
  28.5 3.4 %select_convert_fusion.1 = bf16[8,5,256,256]{3,2,1,0:T(8,128)(2,1)S(1)} fusion(pred[256,256]{1,0:T(8,128)(4,1)S(1)} %iota_compare_fusion, bf16[8,5,256,128]{3,2,1,0:T(8,128)(2,1)S(1)} %bitcast.95, bf16[8,5,256,128]{3,2,1,0:T(8,128)(2,1)} %bitcast.106), kind=kOutput, calls=%fused_computation.1 | convolution fusion | flops 676331520 | bytes 10551296 | tf_op jit(solution)/shard_map/hnid,hnjd->hnij/dot_general | solution.py:67
  31.9 4.0 %fusion.35 = f32[8,5,256,128]{3,2,1,0:T(8,128)} fusion(bf16[8,5,256,256]{3,2,1,0:T(8,128)(2,1)S(1)} %select_convert_fusion.1, bf16[8,5,256,128]{3,2,1,0:T(8,128)(2,1)S(1)} %bitcast.110), kind=kOutput, calls=%fused_computation.61 | convolution fusion | flops 671088640 | bytes 13107200 | tf_op jit(solution)/shard_map/hnij,hnjd->hnid/dot_general | solution.py:71
  37.2 2.1 %collective-permute-done.1 = f32[8,128,128]{2,1,0:T(8,128)S(1)} collective-permute-done((f32[8,128,128]{2,1,0:T(8,128)}, f32[8,128,128]{2,1,0:T(8,128)S(1)}, u32[]{:S(2)}, u32[]{:S(2)}) %collective-permute-start.1) | collective-permute-done | bytes 524320 | tf_op jit(solution)/shard_map/ppermute | solution.py:17
  39.3 1.9 %multiply_add_fusion.3 = f32[8,128,128]{2,1,0:T(8,128)} fusion(f32[8,128,128]{2,1,0:T(8,128)} %bitcast.11, f32[8,128,128]{2,1,0:T(8,128)S(1)} %collective-permute-done.1, f32[]{:T(128)S(6)} %convert_element_type.66, pred[]{:T(512)S(6)} %ge.12), kind=kLoop, calls=%fused_computation.28 | loop fusion | flops 393216 | bytes 1572869 | tf_op jit(solution)/shard_map/add | solution.py:21
  41.2 4.8 %collective-permute-start.3 = (f32[8,128,128]{2,1,0:T(8,128)}, f32[8,128,128]{2,1,0:T(8,128)}, u32[]{:S(2)}, u32[]{:S(2)}) collective-permute-start(f32[8,128,128]{2,1,0:T(8,128)} %multiply_add_fusion.3), channel_id=1, source_target_pairs={{0,8},{4,12},{1,9},{5,13},{2,10},{6,14},{3,11},{7,15},{16,24},{20,... | collective-permute-start | bytes 1572872 | tf_op jit(solution)/shard_map/ppermute | solution.py:17
  46.0 7.2 %fusion.8 = f32[8,128,128,5]{2,3,1,0:T(8,128)} fusion(f32[8,5,128,128]{3,2,1,0:T(8,128)} %copy-done.2, f32[5]{0:T(128)S(1)} %convert_element_type.63), kind=kOutput, calls=%fused_computation.18 | convolution fusion | flops 39321676 | bytes 5242900 | tf_op jit(solution)/shard_map/bc,hcde->hbde/dot_general | solution.py:74
  55.8 3.0 %fusion.11 = bf16[8,5,128,128]{3,2,1,0:T(8,128)(2,1)S(1)} fusion(f32[8,128,128,5]{2,3,1,0:T(8,128)} %fusion.8, f32[8,128,128]{2,1,0:T(8,128)S(1)} %multiply_add_fusion.2, f32[5]{0:T(128)S(1)} %get-tuple-element.6), kind=kLoop, calls=%fused_computation.23 | loop fusion | flops 1966080 | bytes 4456468 | tf_op jit(solution)/shard_map/convert_element_type | solution.py:79
  63.1 10.3 %psum.7 = f32[2,1280]{1,0:T(2,128)S(1)} all-reduce(f32[2,1280]{1,0:T(2,128)S(1)} %pad_maximum_fusion), channel_id=1, replica_groups=mesh['groups'=2,'ctx'=4,'sub'=2,'head'=2] {'sub','head'}, use_global_device_ids=true, to_apply=%region_2.3 | all-reduce | flops 2560 | bytes 20480 | tf_op jit(solution)/shard_map/psum | solution.py:89
  73.5 4.0 %fusion.5 = bf16[8,1280,128]{2,1,0:T(8,128)(2,1)S(1)} fusion(f32[8,5,256,128]{3,2,1,0:T(8,128)} %copy-done.1, bf16[8,1280,128]{2,1,0:T(8,128)(2,1)} %param.9, f32[1280]{0:T(1024)S(1)} %get-tuple-element.4, f32[1280]{0:T(1024)S(1)} %multiply_divide_fusion, f32[8,128]{1,0:T(8,128)S(1)} %copy-done.15), kind=kLoop, calls=%fused_computation.11 | loop fusion | flops 7864320 | bytes 10500096 | tf_op jit(solution)/shard_map/convert_element_type | solution.py:93
  77.5 7.4 %fusion.39 = f32[8,5,256,128]{3,2,1,0:T(8,128)} fusion(bf16[8,5,256,256]{3,2,1,0:T(8,128)(2,1)} %copy-done.6, bf16[8,5,256,128]{3,2,1,0:T(8,128)(2,1)S(1)} %bitcast.99), kind=kOutput, calls=%fused_computation.65 | convolution fusion | flops 671088640 | bytes 13107200 | tf_op jit(solution)/shard_map/hnij,hnid->hnjd/dot_general | solution.py:115
  84.9 2.4 %convolution_bitcast_fusion = f32[8,5,128,128]{2,3,1,0:T(8,128)} fusion(bf16[8,5,256,128]{3,2,1,0:T(8,128)(2,1)S(1)} %bitcast.100, bf16[8,5,256,128]{3,2,1,0:T(8,128)(2,1)S(1)} %bitcast.98), kind=kOutput, calls=%fused_computation.24 | convolution fusion | flops 335544320 | bytes 7864320 | tf_op jit(solution)/shard_map/hnid,hnie->hnde/dot_general | solution.py:97
  87.3 3.9 %select_convert_fusion = bf16[8,5,256,256]{3,2,1,0:T(8,128)(2,1)} fusion(pred[256,256]{1,0:T(8,128)(4,1)S(1)} %iota_compare_fusion, bf16[8,5,256,128]{3,2,1,0:T(8,128)(2,1)S(1)} %bitcast.101, bf16[8,5,256,128]{3,2,1,0:T(8,128)(2,1)S(1)} %bitcast.111), kind=kOutput, calls=%fused_computation | convolution fusion | flops 676331520 | bytes 10551296 | tf_op jit(solution)/shard_map/hnid,hnjd->hnij/dot_general | solution.py:105
  91.2 4.7 %copy.29 = f32[8,5,128,128]{3,1,2,0:T(8,128)} copy(f32[8,5,128,128]{2,3,1,0:T(8,128)} %convolution_bitcast_fusion) | data formatting | bytes 5242880 | tf_op jit(solution)/shard_map/hnid,hnie->hnde/dot_general | solution.py:97
  95.9 5.2 %fusion.25 = f32[1,8,128,128]{3,0,2,1:T(1,128)S(1)} fusion(f32[8,5,128,128]{3,1,2,0:T(8,128)} %copy.29, f32[]{:T(128)} %bitcast.21, s32[5]{0:T(128)S(1)} %copy-done.16), kind=kOutput, calls=%fused_computation.49 | convolution fusion | flops 7864330 | bytes 3145752 | tf_op jit(solution)/shard_map/c,hcde->hde/dot_general | solution.py:101
  101.1 1.4 collective-permute-start.5
  102.5 4.2 %fusion.38 = f32[8,5,256,128]{3,2,1,0:T(8,128)S(1)} fusion(bf16[8,5,256,256]{3,2,1,0:T(8,128)(2,1)} %select_convert_fusion, bf16[8,5,256,128]{3,2,1,0:T(8,128)(2,1)S(1)} %bitcast.97), kind=kOutput, calls=%fused_computation.64 | convolution fusion | flops 671088640 | bytes 13107200 | tf_op jit(solution)/shard_map/hnij,hnid->hnjd/dot_general | solution.py:112
  106.8 1.5 fusion.37
  108.3 17.3 %collective-permute-done.5 = f32[8,128,128]{2,1,0:T(8,128)S(1)} collective-permute-done((f32[8,128,128]{2,1,0:T(8,128)S(1)}, f32[8,128,128]{2,1,0:T(8,128)S(1)}, u32[]{:S(2)}, u32[]{:S(2)}) %collective-permute-start.5) | collective-permute-done | bytes 524320 | tf_op jit(solution)/shard_map/ppermute | solution.py:17
  125.6 1.8 %collective-permute-start.7 = (f32[8,128,128]{2,1,0:T(8,128)S(1)}, f32[8,128,128]{2,1,0:T(8,128)S(1)}, u32[]{:S(2)}, u32[]{:S(2)}) collective-permute-start(f32[8,128,128]{2,1,0:T(8,128)S(1)} %multiply_add_fusion.1), channel_id=1, source_target_pairs={{8,0},{12,4},{9,1},{13,5},{10,2},{14,6},{11,3},{15,7},{24,16},{28,... | collective-permute-start | bytes 1572872 | tf_op jit(solution)/shard_map/ppermute | solution.py:17
  127.5 2.2 %fusion.19 = f32[8,128,128,5]{2,3,1,0:T(8,128)S(1)} fusion(f32[8,5,128,128]{3,1,2,0:T(8,128)S(1)} %copy-done.5, f32[5]{0:T(128)S(1)} %convert_element_type.63), kind=kOutput, calls=%fused_computation.44 | convolution fusion | flops 39321676 | bytes 5242900 | tf_op jit(solution)/shard_map/bc,hcde->hbde/dot_general | solution.py:118
  129.7 2.4 %add_convert_fusion = bf16[8,5,256,128]{3,2,1,0:T(8,128)(2,1)} fusion(f32[8,5,256,128]{3,2,1,0:T(8,128)S(1)} %fusion.37, bf16[8,5,256,128]{3,2,1,0:T(8,128)(2,1)S(1)} %bitcast.102, bf16[8,5,128,128]{3,2,1,0:T(8,128)(2,1)S(1)} %copy-done.13), kind=kOutput, calls=%fused_computation.13 | convolution fusion | flops 338165760 | bytes 11796480 | tf_op jit(solution)/shard_map/hnie,hnde->hnid/dot_general | solution.py:124
  132.2 21.3 %collective-permute-done.7 = f32[8,128,128]{2,1,0:T(8,128)S(1)} collective-permute-done((f32[8,128,128]{2,1,0:T(8,128)S(1)}, f32[8,128,128]{2,1,0:T(8,128)S(1)}, u32[]{:S(2)}, u32[]{:S(2)}) %collective-permute-start.7) | collective-permute-done | bytes 524320 | tf_op jit(solution)/shard_map/ppermute | solution.py:17
  154.2 2.4 %fusion = bf16[8,5,256,128]{3,2,1,0:T(8,128)(2,1)} fusion(f32[8,5,256,128]{3,2,1,0:T(8,128)S(1)} %bitcast.114, bf16[8,5,256,128]{3,2,1,0:T(8,128)(2,1)S(1)} %bitcast.108, bf16[8,5,128,128]{3,2,1,0:T(8,128)(2,1)S(1)} %fusion.10), kind=kOutput, calls=%fused_computation.3 | convolution fusion | flops 338165760 | bytes 11796480 | tf_op jit(solution)/shard_map/hnid,hnde->hnie/dot_general | solution.py:130
  156.6 2.4 %fusion.1 = bf16[8,5,256,128]{3,2,1,0:T(8,128)(2,1)} fusion(f32[8,5,256,128]{3,2,1,0:T(8,128)S(1)} %fusion.38, bf16[8,5,128,128]{3,2,1,0:T(8,128)(2,1)S(1)} %fusion.10, bf16[8,5,256,128]{3,2,1,0:T(8,128)(2,1)S(1)} %bitcast.112), kind=kOutput, calls=%fused_computation.5 | convolution fusion | flops 338165760 | bytes 11796480 | tf_op jit(solution)/shard_map/hnie,hnde->hnid/dot_general | solution.py:127
  (63 shorter events, 6.7 us)
Async XLA Ops:
  0.6 27.8 %copy-start = (bf16[8,1280,128]{2,1,0:T(8,128)(2,1)S(1)}, bf16[8,1280,128]{2,1,0:T(8,128)(2,1)}, u32[]{:S(2)}) copy-start(bf16[8,1280,128]{2,1,0:T(8,128)(2,1)} %param.6) | copy-start | bytes 7864324
  2.0 52.4 %collective-permute-start.6 = (f32[]{:T(128)}, f32[]{:T(128)}, u32[]{:S(2)}, u32[]{:S(2)}) collective-permute-start(f32[]{:T(128)} %bitcast.21), channel_id=1, source_target_pairs={{8,0},{12,4},{9,1},{13,5},{10,2},{14,6},{11,3},{15,7},{24,16},{28,... | collective-permute-start | bytes 20 | tf_op jit(solution)/shard_map/ppermute | solution.py:17
  3.3 49.9 %collective-permute-start.4 = (f32[]{:T(128)}, f32[]{:T(128)}, u32[]{:S(2)}, u32[]{:S(2)}) collective-permute-start(f32[]{:T(128)} %bitcast.21), channel_id=1, source_target_pairs={{4,0},{8,4},{12,8},{5,1},{9,5},{13,9},{6,2},{10,6},{14,10},{7,3},{... | collective-permute-start | bytes 20 | tf_op jit(solution)/shard_map/ppermute | solution.py:17
  4.6 50.5 %collective-permute-start.2 = (f32[]{:T(128)}, f32[]{:T(128)}, u32[]{:S(2)}, u32[]{:S(2)}) collective-permute-start(f32[]{:T(128)} %bitcast.7), channel_id=1, source_target_pairs={{0,8},{4,12},{1,9},{5,13},{2,10},{6,14},{3,11},{7,15},{16,24},{20,... | collective-permute-start | bytes 20 | tf_op jit(solution)/shard_map/ppermute | solution.py:17
  12.2 23.7 %collective-permute-start = (f32[]{:T(128)}, f32[]{:T(128)}, u32[]{:S(2)}, u32[]{:S(2)}) collective-permute-start(f32[]{:T(128)} %bitcast.7), channel_id=1, source_target_pairs={{0,4},{4,8},{8,12},{1,5},{5,9},{9,13},{2,6},{6,10},{10,14},{3,7},{... | collective-permute-start | bytes 20 | tf_op jit(solution)/shard_map/ppermute | solution.py:17
  17.2 4.9 %copy-start.16 = (s32[5]{0:T(128)S(1)}, s32[5]{0:T(128)}, u32[]{:S(2)}) copy-start(s32[5]{0:T(128)} %param.11) | copy-start | bytes 64
  20.6 1.5 copy-start.2
  27.0 12.3 %collective-permute-start.1 = (f32[8,128,128]{2,1,0:T(8,128)}, f32[8,128,128]{2,1,0:T(8,128)S(1)}, u32[]{:S(2)}, u32[]{:S(2)}) collective-permute-start(f32[8,128,128]{2,1,0:T(8,128)} %bitcast.11), channel_id=1, source_target_pairs={{0,4},{4,8},{8,12},{1,5},{5,9},{9,13},{2,6},{6,10},{10,14},{3,7},{... | collective-permute-start | bytes 1572872 | tf_op jit(solution)/shard_map/ppermute | solution.py:17
  28.5 3.4 %copy-start.9 = (bf16[8,1280,128]{2,1,0:T(8,128)(2,1)S(1)}, bf16[8,1280,128]{2,1,0:T(8,128)(2,1)}, u32[]{:S(2)}) copy-start(bf16[8,1280,128]{2,1,0:T(8,128)(2,1)} %param.8) | copy-start | bytes 7864324
  31.9 4.0 %copy-start.6 = (bf16[8,5,256,256]{3,2,1,0:T(8,128)(2,1)}, bf16[8,5,256,256]{3,2,1,0:T(8,128)(2,1)S(1)}, u32[]{:S(2)}) copy-start(bf16[8,5,256,256]{3,2,1,0:T(8,128)(2,1)S(1)} %select_convert_fusion.1) | copy-start | bytes 15728644
  41.2 14.5 %collective-permute-start.3 = (f32[8,128,128]{2,1,0:T(8,128)}, f32[8,128,128]{2,1,0:T(8,128)}, u32[]{:S(2)}, u32[]{:S(2)}) collective-permute-start(f32[8,128,128]{2,1,0:T(8,128)} %multiply_add_fusion.3), channel_id=1, source_target_pairs={{0,8},{4,12},{1,9},{5,13},{2,10},{6,14},{3,11},{7,15},{16,24},{20,... | collective-permute-start | bytes 1572872 | tf_op jit(solution)/shard_map/ppermute | solution.py:17
  55.8 3.7 %copy-start.7 = (f32[8,5,256,128]{3,2,1,0:T(8,128)S(1)}, f32[8,5,256,128]{3,2,1,0:T(8,128)}, u32[]{:S(2)}) copy-start(f32[8,5,256,128]{3,2,1,0:T(8,128)} %fusion.35) | copy-start | bytes 15728644
  59.5 1.2 copy-start.12
  59.5 2.3 %copy-start.14 = (bf16[8,1280,128]{2,1,0:T(8,128)(2,1)S(1)}, bf16[8,1280,128]{2,1,0:T(8,128)(2,1)}, u32[]{:S(2)}) copy-start(bf16[8,1280,128]{2,1,0:T(8,128)(2,1)} %param.9) | copy-start | bytes 7864324
  59.5 2.3 %copy-start.15 = (f32[8,128]{1,0:T(8,128)S(1)}, f32[8,128]{1,0:T(8,128)}, u32[]{:S(2)}) copy-start(f32[8,128]{1,0:T(8,128)} %param.10) | copy-start | bytes 12292
  60.7 2.4 %copy-start.1 = (f32[8,5,256,128]{3,2,1,0:T(8,128)}, f32[8,5,256,128]{3,2,1,0:T(8,128)S(1)}, u32[]{:S(2)}) copy-start(f32[8,5,256,128]{3,2,1,0:T(8,128)S(1)} %get-tuple-element.10) | copy-start | bytes 15728644
  77.5 9.8 %copy-start.3 = (bf16[8,1280,128]{2,1,0:T(8,128)(2,1)}, bf16[8,1280,128]{2,1,0:T(8,128)(2,1)S(1)}, u32[]{:S(2)}) copy-start(bf16[8,1280,128]{2,1,0:T(8,128)(2,1)S(1)} %fusion.5) | copy-start | bytes 7864324
  84.9 2.4 %copy-start.10 = (bf16[8,1280,128]{2,1,0:T(8,128)(2,1)S(1)}, bf16[8,1280,128]{2,1,0:T(8,128)(2,1)}, u32[]{:S(2)}) copy-start(bf16[8,1280,128]{2,1,0:T(8,128)(2,1)} %param.8) | copy-start | bytes 7864324
  95.9 10.9 %slice-start = ((s8[5242880]{0:T(1024)(128)(4,1)}), s8[4194304]{0:T(1024)(128)(4,1)S(1)}, s32[]{:S(2)}) async-start(s8[5242880]{0:T(1024)(128)(4,1)} %bitcast.103), calls=%async_computation | async-start | bytes 8388608
  101.1 5.7 %slice-start.1 = ((s8[5242880]{0:T(1024)(128)(4,1)}), s8[1048576]{0:T(1024)(128)(4,1)S(1)}, s32[]{:S(2)}) async-start(s8[5242880]{0:T(1024)(128)(4,1)} %bitcast.103), calls=%async_computation.1 | async-start | bytes 2097152
  101.1 24.5 %collective-permute-start.5 = (f32[8,128,128]{2,1,0:T(8,128)S(1)}, f32[8,128,128]{2,1,0:T(8,128)S(1)}, u32[]{:S(2)}, u32[]{:S(2)}) collective-permute-start(f32[8,128,128]{2,1,0:T(8,128)S(1)} %bitcast.118), channel_id=1, source_target_pairs={{4,0},{8,4},{12,8},{5,1},{9,5},{13,9},{6,2},{10,6},{14,10},{7,3},{... | collective-permute-start | bytes 1572872 | tf_op jit(solution)/shard_map/ppermute | solution.py:17
  102.5 4.2 %copy-start.8 = (bf16[8,1280,128]{2,1,0:T(8,128)(2,1)S(1)}, bf16[8,1280,128]{2,1,0:T(8,128)(2,1)}, u32[]{:S(2)}) copy-start(bf16[8,1280,128]{2,1,0:T(8,128)(2,1)} %param.7) | copy-start | bytes 7864324
  106.8 20.7 %copy-start.5 = (f32[8,5,128,128]{3,1,2,0:T(8,128)S(1)}, f32[8,5,128,128]{3,1,2,0:T(8,128)}, u32[]{:S(2)}) copy-start(f32[8,5,128,128]{3,1,2,0:T(8,128)} %copy.29) | copy-start | bytes 7864324
  125.6 4.1 %copy-start.4 = (bf16[8,1280,128]{2,1,0:T(8,128)(2,1)S(1)}, bf16[8,1280,128]{2,1,0:T(8,128)(2,1)}, u32[]{:S(2)}) copy-start(bf16[8,1280,128]{2,1,0:T(8,128)(2,1)} %copy-done.3) | copy-start | bytes 7864324
  125.6 4.1 %copy-start.13 = (bf16[8,5,128,128]{3,2,1,0:T(8,128)(2,1)S(1)}, bf16[8,5,128,128]{3,2,1,0:T(8,128)(2,1)}, u32[]{:S(2)}) copy-start(bf16[8,5,128,128]{3,2,1,0:T(8,128)(2,1)} %copy-done.12) | copy-start | bytes 3932164
  125.6 27.8 %collective-permute-start.7 = (f32[8,128,128]{2,1,0:T(8,128)S(1)}, f32[8,128,128]{2,1,0:T(8,128)S(1)}, u32[]{:S(2)}, u32[]{:S(2)}) collective-permute-start(f32[8,128,128]{2,1,0:T(8,128)S(1)} %multiply_add_fusion.1), channel_id=1, source_target_pairs={{8,0},{12,4},{9,1},{13,5},{10,2},{14,6},{11,3},{15,7},{24,16},{28,... | collective-permute-start | bytes 1572872 | tf_op jit(solution)/shard_map/ppermute | solution.py:17
  127.5 26.7 %slice-start.2 = ((s8[5242880]{0:T(1024)(128)(4,1)}), s8[4194304]{0:T(1024)(128)(4,1)S(1)}, s32[]{:S(2)}) async-start(s8[5242880]{0:T(1024)(128)(4,1)} %bitcast.113), calls=%async_computation.2 | async-start | bytes 8388608
  129.7 24.5 %slice-start.3 = ((s8[5242880]{0:T(1024)(128)(4,1)}), s8[1048576]{0:T(1024)(128)(4,1)S(1)}, s32[]{:S(2)}) async-start(s8[5242880]{0:T(1024)(128)(4,1)} %bitcast.113), calls=%async_computation.3 | async-start | bytes 2097152
  154.2 2.4 %copy-start.11 = (bf16[8,1280,128]{2,1,0:T(8,128)(2,1)S(1)}, bf16[8,1280,128]{2,1,0:T(8,128)(2,1)}, u32[]{:S(2)}) copy-start(bf16[8,1280,128]{2,1,0:T(8,128)(2,1)} %param.8) | copy-start | bytes 7864324
where the time goes:
time: 160 us; the launch traced here: 159 us
  matrix products  58.1 us (36%)
  waiting for transfers between devices  40.7 us (25%)
  starting transfers between devices  24.5 us (15%)
  other arithmetic  11.4 us (7%)
  blocking collectives  10.3 us (6%)
  local copies, waits for them, and re-layouts  9.19 us (6%)
  between operations  4.79 us (3%)
    ppermute x8, waiting for transfers between devices, shift(): return lax.ppermute(value, axis, pairs)  40.7 us
    ppermute x8, starting transfers between devices, shift(): return lax.ppermute(value, axis, pairs)  24.5 us
    psum x1, blocking collectives, on_device(): total_sums = lax.psum(local_sums, ('sub', 'head'))  10.3 us
    dot_general x1, matrix products, on_device(): jnp.einsum('hnij,hnid->hnjd', block_probs, output_grad_blocks, preferred_...  7.37 us
    dot_general x1, matrix products, on_device(): jnp.einsum('bc,hcde->hbde', earlier_mask, key_value_block, precision=high...  7.22 us
    dot_general x1, matrix products, on_device(): jnp.einsum('c,hcde->hde', first_match, query_grad_block, precision=highes...  5.18 us
    dot_general x1, matrix products, on_device(): jnp.einsum('c,hcde->hde', last_match, key_value_block, precision=highest_...  4.89 us
    dot_general x1, local copies, waits for them, and re-layouts, on_device(): jnp.einsum('hnid,hnie->hnde', query_blocks, output_grad_blocks, preferred...  4.7 us
  transfers between devices with their start and end apart: 8, of which 3 were waited for; matrix products, arithmetic and copies ran while one was open for 22% of the time, Pallas kernels for 0%

commit v1 on v0

--- a/solution.py
+++ b/solution.py
@@ -86,7 +86,7 @@
     local_sums = jnp.stack(
         [jnp.sum(raw_attn * raw_attn, axis=(0, 2)), jnp.sum(scaled * raw_attn, axis=(0, 2))]
     )
-    total_sums = lax.psum(local_sums, ("sub", "head"))
+    total_sums = jnp.sum(lax.all_gather(local_sums, ("sub", "head")), axis=0)
     root_mean = jnp.sqrt(total_sums[0] / feature_count + 1e-06)
     inner_mean = total_sums[1] / feature_count
     factor = inner_mean / (root_mean * root_mean)

time: 160 us -> 156 us (0.975)
  blocking collectives: 10.3 us -> 5.63 us
    psum x1 -> x0, blocking collectives: 10.3 us -> none  [on_device(): total_sums = lax.psum(local_sums, ('sub', 'head'))]
    all_gather x0 -> x1, blocking collectives: none -> 5.63 us  [on_device(): total_sums = jnp.sum(lax.all_gather(local_sums, ('sub', 'head')), axis=0)]
  transfers between devices with their start and end apart: 8 -> 8, of which waited for: 3 -> 3; matrix products, arithmetic and copies ran while one was open for 22% -> 23% of each run, Pallas kernels for 0% -> 0%
where the time goes in v1:
time: 156 us; the launch traced here: 155 us
  matrix products  58.1 us (37%)
  waiting for transfers between devices  41.8 us (27%)
  starting transfers between devices  24.5 us (16%)
  other arithmetic  11.4 us (7%)
  local copies, waits for them, and re-layouts  9.19 us (6%)
  blocking collectives  5.63 us (4%)
  between operations  4.79 us (3%)
    ppermute x8, waiting for transfers between devices, shift(): return lax.ppermute(value, axis, pairs)  41.8 us
    ppermute x8, starting transfers between devices, shift(): return lax.ppermute(value, axis, pairs)  24.5 us
    dot_general x1, matrix products, on_device(): jnp.einsum('hnij,hnid->hnjd', block_probs, output_grad_blocks, preferred_...  7.38 us
    dot_general x1, matrix products, on_device(): jnp.einsum('bc,hcde->hbde', earlier_mask, key_value_block, precision=high...  7.22 us
    all_gather x1, blocking collectives, on_device(): total_sums = jnp.sum(lax.all_gather(local_sums, ('sub', 'head')), axis=0)  5.63 us
    dot_general x1, matrix products, on_device(): jnp.einsum('c,hcde->hde', first_match, query_grad_block, precision=highes...  5.18 us
    dot_general x1, matrix products, on_device(): jnp.einsum('c,hcde->hde', last_match, key_value_block, precision=highest_...  4.89 us
    dot_general x1, local copies, waits for them, and re-layouts, on_device(): jnp.einsum('hnid,hnie->hnde', query_blocks, output_grad_blocks, preferred...  4.7 us
  transfers between devices with their start and end apart: 8, of which 3 were waited for; matrix products, arithmetic and copies ran while one was open for 23% of the time, Pallas kernels for 0%

profile of v1, /device:TPU:0, one launch (start us, length us, event | category | flops | bytes accessed | tf_op | source)
XLA Modules:
  0.0 155.5 jit_solution(3425827465993729216)
XLA Ops:
  2.0 1.3 collective-permute-start.6
  3.3 1.3 collective-permute-start.4
  4.6 7.6 %collective-permute-start.2 = (f32[]{:T(128)}, f32[]{:T(128)}, u32[]{:S(2)}, u32[]{:S(2)}) collective-permute-start(f32[]{:T(128)} %bitcast.7), channel_id=1, source_target_pairs={{0,8},{4,12},{1,9},{5,13},{2,10},{6,14},{3,11},{7,15},{16,24},{20,... | collective-permute-start | bytes 20 | tf_op jit(solution)/shard_map/ppermute | solution.py:17
  12.2 5.0 %collective-permute-start = (f32[]{:T(128)}, f32[]{:T(128)}, u32[]{:S(2)}, u32[]{:S(2)}) collective-permute-start(f32[]{:T(128)} %bitcast.7), channel_id=1, source_target_pairs={{0,4},{4,8},{8,12},{1,5},{5,9},{9,13},{2,6},{6,10},{10,14},{3,7},{... | collective-permute-start | bytes 20 | tf_op jit(solution)/shard_map/ppermute | solution.py:17
  17.2 3.4 %fusion.36 = f32[8,5,128,128]{3,2,1,0:T(8,128)S(1)} fusion(bf16[8,5,256,128]{3,2,1,0:T(8,128)(2,1)} %bitcast.107, bf16[8,5,256,128]{3,2,1,0:T(8,128)(2,1)} %bitcast.111), kind=kOutput, calls=%fused_computation.62 | convolution fusion | flops 335544320 | bytes 7864320 | tf_op jit(solution)/shard_map/hnid,hnie->hnde/dot_general | solution.py:61
  20.6 1.5 copy-done.2
  22.1 4.9 %fusion.6 = f32[1,8,128,128]{3,0,2,1:T(1,128)} fusion(f32[8,5,128,128]{3,2,1,0:T(8,128)S(1)} %fusion.36, f32[]{:T(128)} %bitcast.7, s32[5]{0:T(128)S(1)} %copy-done.16), kind=kOutput, calls=%fused_computation.16 | convolution fusion | flops 7864330 | bytes 3145752 | tf_op jit(solution)/shard_map/c,hcde->hde/dot_general | solution.py:65
  27.0 1.4 collective-permute-start.1
  28.5 3.4 %select_convert_fusion.1 = bf16[8,5,256,256]{3,2,1,0:T(8,128)(2,1)S(1)} fusion(pred[256,256]{1,0:T(8,128)(4,1)S(1)} %iota_compare_fusion, bf16[8,5,256,128]{3,2,1,0:T(8,128)(2,1)S(1)} %bitcast.97, bf16[8,5,256,128]{3,2,1,0:T(8,128)(2,1)} %bitcast.108), kind=kOutput, calls=%fused_computation.1 | convolution fusion | flops 676331520 | bytes 10551296 | tf_op jit(solution)/shard_map/hnid,hnjd->hnij/dot_general | solution.py:67
  31.9 4.0 %fusion.35 = f32[8,5,256,128]{3,2,1,0:T(8,128)} fusion(bf16[8,5,256,256]{3,2,1,0:T(8,128)(2,1)S(1)} %select_convert_fusion.1, bf16[8,5,256,128]{3,2,1,0:T(8,128)(2,1)S(1)} %bitcast.112), kind=kOutput, calls=%fused_computation.61 | convolution fusion | flops 671088640 | bytes 13107200 | tf_op jit(solution)/shard_map/hnij,hnjd->hnid/dot_general | solution.py:71
  37.2 2.1 %collective-permute-done.1 = f32[8,128,128]{2,1,0:T(8,128)S(1)} collective-permute-done((f32[8,128,128]{2,1,0:T(8,128)}, f32[8,128,128]{2,1,0:T(8,128)S(1)}, u32[]{:S(2)}, u32[]{:S(2)}) %collective-permute-start.1) | collective-permute-done | bytes 524320 | tf_op jit(solution)/shard_map/ppermute | solution.py:17
  39.3 1.9 %multiply_add_fusion.3 = f32[8,128,128]{2,1,0:T(8,128)} fusion(f32[8,128,128]{2,1,0:T(8,128)} %bitcast.11, f32[8,128,128]{2,1,0:T(8,128)S(1)} %collective-permute-done.1, f32[]{:T(128)S(6)} %convert_element_type.66, pred[]{:T(512)S(6)} %ge.12), kind=kLoop, calls=%fused_computation.28 | loop fusion | flops 393216 | bytes 1572869 | tf_op jit(solution)/shard_map/add | solution.py:21
  41.2 4.8 %collective-permute-start.3 = (f32[8,128,128]{2,1,0:T(8,128)}, f32[8,128,128]{2,1,0:T(8,128)}, u32[]{:S(2)}, u32[]{:S(2)}) collective-permute-start(f32[8,128,128]{2,1,0:T(8,128)} %multiply_add_fusion.3), channel_id=1, source_target_pairs={{0,8},{4,12},{1,9},{5,13},{2,10},{6,14},{3,11},{7,15},{16,24},{20,... | collective-permute-start | bytes 1572872 | tf_op jit(solution)/shard_map/ppermute | solution.py:17
  46.0 7.2 %fusion.8 = f32[8,128,128,5]{2,3,1,0:T(8,128)} fusion(f32[8,5,128,128]{3,2,1,0:T(8,128)} %copy-done.2, f32[5]{0:T(128)S(1)} %convert_element_type.63), kind=kOutput, calls=%fused_computation.18 | convolution fusion | flops 39321676 | bytes 5242900 | tf_op jit(solution)/shard_map/bc,hcde->hbde/dot_general | solution.py:74
  55.8 3.0 %fusion.11 = bf16[8,5,128,128]{3,2,1,0:T(8,128)(2,1)S(1)} fusion(f32[8,128,128,5]{2,3,1,0:T(8,128)} %fusion.8, f32[8,128,128]{2,1,0:T(8,128)S(1)} %multiply_add_fusion.2, f32[5]{0:T(128)S(1)} %get-tuple-element.6), kind=kLoop, calls=%fused_computation.23 | loop fusion | flops 1966080 | bytes 4456468 | tf_op jit(solution)/shard_map/convert_element_type | solution.py:79
  63.1 5.6 %all-gather.1 = f32[4,2,1280]{2,1,0:T(2,128)S(1)} all-gather(f32[1,2,1280]{2,1,0:T(2,128)S(1)} %maximum_bitcast_fusion), channel_id=2, replica_groups=mesh['groups'=2,'ctx'=4,'sub'=2,'head'=2] {'sub','head'}, dimensions={0}, use_global_device_ids=true | all-gather | bytes 51200 | tf_op jit(solution)/shard_map/all_gather | solution.py:89
  68.8 4.0 %fusion.5 = bf16[8,1280,128]{2,1,0:T(8,128)(2,1)S(1)} fusion(f32[8,5,256,128]{3,2,1,0:T(8,128)} %copy-done.1, bf16[8,1280,128]{2,1,0:T(8,128)(2,1)} %param.9, f32[1280]{0:T(1024)S(1)} %get-tuple-element.4, f32[1280]{0:T(1024)S(1)} %multiply_divide_fusion, f32[8,128]{1,0:T(8,128)S(1)} %copy-done.15), kind=kLoop, calls=%fused_computation.11 | loop fusion | flops 7864320 | bytes 10500096 | tf_op jit(solution)/shard_map/convert_element_type | solution.py:93
  72.9 7.4 %fusion.39 = f32[8,5,256,128]{3,2,1,0:T(8,128)} fusion(bf16[8,5,256,256]{3,2,1,0:T(8,128)(2,1)} %copy-done.6, bf16[8,5,256,128]{3,2,1,0:T(8,128)(2,1)S(1)} %bitcast.101), kind=kOutput, calls=%fused_computation.65 | convolution fusion | flops 671088640 | bytes 13107200 | tf_op jit(solution)/shard_map/hnij,hnid->hnjd/dot_general | solution.py:115
  80.2 2.4 %convolution_bitcast_fusion = f32[8,5,128,128]{2,3,1,0:T(8,128)} fusion(bf16[8,5,256,128]{3,2,1,0:T(8,128)(2,1)S(1)} %bitcast.102, bf16[8,5,256,128]{3,2,1,0:T(8,128)(2,1)S(1)} %bitcast.100), kind=kOutput, calls=%fused_computation.24 | convolution fusion | flops 335544320 | bytes 7864320 | tf_op jit(solution)/shard_map/hnid,hnie->hnde/dot_general | solution.py:97
  82.6 3.9 %select_convert_fusion = bf16[8,5,256,256]{3,2,1,0:T(8,128)(2,1)} fusion(pred[256,256]{1,0:T(8,128)(4,1)S(1)} %iota_compare_fusion, bf16[8,5,256,128]{3,2,1,0:T(8,128)(2,1)S(1)} %bitcast.103, bf16[8,5,256,128]{3,2,1,0:T(8,128)(2,1)S(1)} %bitcast.113), kind=kOutput, calls=%fused_computation | convolution fusion | flops 676331520 | bytes 10551296 | tf_op jit(solution)/shard_map/hnid,hnjd->hnij/dot_general | solution.py:105
  86.5 4.7 %copy.42 = f32[8,5,128,128]{3,1,2,0:T(8,128)} copy(f32[8,5,128,128]{2,3,1,0:T(8,128)} %convolution_bitcast_fusion) | data formatting | bytes 5242880 | tf_op jit(solution)/shard_map/hnid,hnie->hnde/dot_general | solution.py:97
  91.2 5.2 %fusion.25 = f32[1,8,128,128]{3,0,2,1:T(1,128)S(1)} fusion(f32[8,5,128,128]{3,1,2,0:T(8,128)} %copy.42, f32[]{:T(128)} %bitcast.22, s32[5]{0:T(128)S(1)} %copy-done.16), kind=kOutput, calls=%fused_computation.49 | convolution fusion | flops 7864330 | bytes 3145752 | tf_op jit(solution)/shard_map/c,hcde->hde/dot_general | solution.py:101
  96.4 1.4 collective-permute-start.5
  97.8 4.2 %fusion.38 = f32[8,5,256,128]{3,2,1,0:T(8,128)S(1)} fusion(bf16[8,5,256,256]{3,2,1,0:T(8,128)(2,1)} %select_convert_fusion, bf16[8,5,256,128]{3,2,1,0:T(8,128)(2,1)S(1)} %bitcast.99), kind=kOutput, calls=%fused_computation.64 | convolution fusion | flops 671088640 | bytes 13107200 | tf_op jit(solution)/shard_map/hnij,hnid->hnjd/dot_general | solution.py:112
  102.1 1.5 fusion.37
  103.6 17.7 %collective-permute-done.5 = f32[8,128,128]{2,1,0:T(8,128)S(1)} collective-permute-done((f32[8,128,128]{2,1,0:T(8,128)S(1)}, f32[8,128,128]{2,1,0:T(8,128)S(1)}, u32[]{:S(2)}, u32[]{:S(2)}) %collective-permute-start.5) | collective-permute-done | bytes 524320 | tf_op jit(solution)/shard_map/ppermute | solution.py:17
  121.4 1.8 %collective-permute-start.7 = (f32[8,128,128]{2,1,0:T(8,128)S(1)}, f32[8,128,128]{2,1,0:T(8,128)S(1)}, u32[]{:S(2)}, u32[]{:S(2)}) collective-permute-start(f32[8,128,128]{2,1,0:T(8,128)S(1)} %multiply_add_fusion.1), channel_id=1, source_target_pairs={{8,0},{12,4},{9,1},{13,5},{10,2},{14,6},{11,3},{15,7},{24,16},{28,... | collective-permute-start | bytes 1572872 | tf_op jit(solution)/shard_map/ppermute | solution.py:17
  123.2 2.2 %fusion.19 = f32[8,128,128,5]{2,3,1,0:T(8,128)S(1)} fusion(f32[8,5,128,128]{3,1,2,0:T(8,128)S(1)} %copy-done.5, f32[5]{0:T(128)S(1)} %convert_element_type.63), kind=kOutput, calls=%fused_computation.44 | convolution fusion | flops 39321676 | bytes 5242900 | tf_op jit(solution)/shard_map/bc,hcde->hbde/dot_general | solution.py:118
  125.5 2.4 %add_convert_fusion = bf16[8,5,256,128]{3,2,1,0:T(8,128)(2,1)} fusion(f32[8,5,256,128]{3,2,1,0:T(8,128)S(1)} %fusion.37, bf16[8,5,256,128]{3,2,1,0:T(8,128)(2,1)S(1)} %bitcast.104, bf16[8,5,128,128]{3,2,1,0:T(8,128)(2,1)S(1)} %copy-done.13), kind=kOutput, calls=%fused_computation.13 | convolution fusion | flops 338165760 | bytes 11796480 | tf_op jit(solution)/shard_map/hnie,hnde->hnid/dot_general | solution.py:124
  127.9 22.0 %collective-permute-done.7 = f32[8,128,128]{2,1,0:T(8,128)S(1)} collective-permute-done((f32[8,128,128]{2,1,0:T(8,128)S(1)}, f32[8,128,128]{2,1,0:T(8,128)S(1)}, u32[]{:S(2)}, u32[]{:S(2)}) %collective-permute-start.7) | collective-permute-done | bytes 524320 | tf_op jit(solution)/shard_map/ppermute | solution.py:17
  150.7 2.4 %fusion = bf16[8,5,256,128]{3,2,1,0:T(8,128)(2,1)} fusion(f32[8,5,256,128]{3,2,1,0:T(8,128)S(1)} %bitcast.116, bf16[8,5,256,128]{3,2,1,0:T(8,128)(2,1)S(1)} %bitcast.110, bf16[8,5,128,128]{3,2,1,0:T(8,128)(2,1)S(1)} %fusion.10), kind=kOutput, calls=%fused_computation.3 | convolution fusion | flops 338165760 | bytes 11796480 | tf_op jit(solution)/shard_map/hnid,hnde->hnie/dot_general | solution.py:130
  153.0 2.4 %fusion.1 = bf16[8,5,256,128]{3,2,1,0:T(8,128)(2,1)} fusion(f32[8,5,256,128]{3,2,1,0:T(8,128)S(1)} %fusion.38, bf16[8,5,128,128]{3,2,1,0:T(8,128)(2,1)S(1)} %fusion.10, bf16[8,5,256,128]{3,2,1,0:T(8,128)(2,1)S(1)} %bitcast.114), kind=kOutput, calls=%fused_computation.5 | convolution fusion | flops 338165760 | bytes 11796480 | tf_op jit(solution)/shard_map/hnie,hnde->hnid/dot_general | solution.py:127
  (64 shorter events, 6.8 us)
Async XLA Ops:
  0.6 27.8 %copy-start = (bf16[8,1280,128]{2,1,0:T(8,128)(2,1)S(1)}, bf16[8,1280,128]{2,1,0:T(8,128)(2,1)}, u32[]{:S(2)}) copy-start(bf16[8,1280,128]{2,1,0:T(8,128)(2,1)} %param.6) | copy-start | bytes 7864324
  2.0 52.4 %collective-permute-start.6 = (f32[]{:T(128)}, f32[]{:T(128)}, u32[]{:S(2)}, u32[]{:S(2)}) collective-permute-start(f32[]{:T(128)} %bitcast.22), channel_id=1, source_target_pairs={{8,0},{12,4},{9,1},{13,5},{10,2},{14,6},{11,3},{15,7},{24,16},{28,... | collective-permute-start | bytes 20 | tf_op jit(solution)/shard_map/ppermute | solution.py:17
  3.3 49.9 %collective-permute-start.4 = (f32[]{:T(128)}, f32[]{:T(128)}, u32[]{:S(2)}, u32[]{:S(2)}) collective-permute-start(f32[]{:T(128)} %bitcast.22), channel_id=1, source_target_pairs={{4,0},{8,4},{12,8},{5,1},{9,5},{13,9},{6,2},{10,6},{14,10},{7,3},{... | collective-permute-start | bytes 20 | tf_op jit(solution)/shard_map/ppermute | solution.py:17
  4.6 50.5 %collective-permute-start.2 = (f32[]{:T(128)}, f32[]{:T(128)}, u32[]{:S(2)}, u32[]{:S(2)}) collective-permute-start(f32[]{:T(128)} %bitcast.7), channel_id=1, source_target_pairs={{0,8},{4,12},{1,9},{5,13},{2,10},{6,14},{3,11},{7,15},{16,24},{20,... | collective-permute-start | bytes 20 | tf_op jit(solution)/shard_map/ppermute | solution.py:17
  12.2 23.7 %collective-permute-start = (f32[]{:T(128)}, f32[]{:T(128)}, u32[]{:S(2)}, u32[]{:S(2)}) collective-permute-start(f32[]{:T(128)} %bitcast.7), channel_id=1, source_target_pairs={{0,4},{4,8},{8,12},{1,5},{5,9},{9,13},{2,6},{6,10},{10,14},{3,7},{... | collective-permute-start | bytes 20 | tf_op jit(solution)/shard_map/ppermute | solution.py:17
  17.2 4.9 %copy-start.16 = (s32[5]{0:T(128)S(1)}, s32[5]{0:T(128)}, u32[]{:S(2)}) copy-start(s32[5]{0:T(128)} %param.11) | copy-start | bytes 64
  20.6 1.5 copy-start.2
  27.0 12.3 %collective-permute-start.1 = (f32[8,128,128]{2,1,0:T(8,128)}, f32[8,128,128]{2,1,0:T(8,128)S(1)}, u32[]{:S(2)}, u32[]{:S(2)}) collective-permute-start(f32[8,128,128]{2,1,0:T(8,128)} %bitcast.11), channel_id=1, source_target_pairs={{0,4},{4,8},{8,12},{1,5},{5,9},{9,13},{2,6},{6,10},{10,14},{3,7},{... | collective-permute-start | bytes 1572872 | tf_op jit(solution)/shard_map/ppermute | solution.py:17
  28.5 3.4 %copy-start.9 = (bf16[8,1280,128]{2,1,0:T(8,128)(2,1)S(1)}, bf16[8,1280,128]{2,1,0:T(8,128)(2,1)}, u32[]{:S(2)}) copy-start(bf16[8,1280,128]{2,1,0:T(8,128)(2,1)} %param.8) | copy-start | bytes 7864324
  31.9 4.0 %copy-start.6 = (bf16[8,5,256,256]{3,2,1,0:T(8,128)(2,1)}, bf16[8,5,256,256]{3,2,1,0:T(8,128)(2,1)S(1)}, u32[]{:S(2)}) copy-start(bf16[8,5,256,256]{3,2,1,0:T(8,128)(2,1)S(1)} %select_convert_fusion.1) | copy-start | bytes 15728644
  41.2 14.5 %collective-permute-start.3 = (f32[8,128,128]{2,1,0:T(8,128)}, f32[8,128,128]{2,1,0:T(8,128)}, u32[]{:S(2)}, u32[]{:S(2)}) collective-permute-start(f32[8,128,128]{2,1,0:T(8,128)} %multiply_add_fusion.3), channel_id=1, source_target_pairs={{0,8},{4,12},{1,9},{5,13},{2,10},{6,14},{3,11},{7,15},{16,24},{20,... | collective-permute-start | bytes 1572872 | tf_op jit(solution)/shard_map/ppermute | solution.py:17
  55.8 3.7 %copy-start.7 = (f32[8,5,256,128]{3,2,1,0:T(8,128)S(1)}, f32[8,5,256,128]{3,2,1,0:T(8,128)}, u32[]{:S(2)}) copy-start(f32[8,5,256,128]{3,2,1,0:T(8,128)} %fusion.35) | copy-start | bytes 15728644
  59.5 1.2 copy-start.12
  59.5 2.3 %copy-start.14 = (bf16[8,1280,128]{2,1,0:T(8,128)(2,1)S(1)}, bf16[8,1280,128]{2,1,0:T(8,128)(2,1)}, u32[]{:S(2)}) copy-start(bf16[8,1280,128]{2,1,0:T(8,128)(2,1)} %param.9) | copy-start | bytes 7864324
  59.5 2.3 %copy-start.15 = (f32[8,128]{1,0:T(8,128)S(1)}, f32[8,128]{1,0:T(8,128)}, u32[]{:S(2)}) copy-start(f32[8,128]{1,0:T(8,128)} %param.10) | copy-start | bytes 12292
  60.7 2.4 %copy-start.1 = (f32[8,5,256,128]{3,2,1,0:T(8,128)}, f32[8,5,256,128]{3,2,1,0:T(8,128)S(1)}, u32[]{:S(2)}) copy-start(f32[8,5,256,128]{3,2,1,0:T(8,128)S(1)} %get-tuple-element.10) | copy-start | bytes 15728644
  72.9 9.8 %copy-start.3 = (bf16[8,1280,128]{2,1,0:T(8,128)(2,1)}, bf16[8,1280,128]{2,1,0:T(8,128)(2,1)S(1)}, u32[]{:S(2)}) copy-start(bf16[8,1280,128]{2,1,0:T(8,128)(2,1)S(1)} %fusion.5) | copy-start | bytes 7864324
  80.2 2.4 %copy-start.10 = (bf16[8,1280,128]{2,1,0:T(8,128)(2,1)S(1)}, bf16[8,1280,128]{2,1,0:T(8,128)(2,1)}, u32[]{:S(2)}) copy-start(bf16[8,1280,128]{2,1,0:T(8,128)(2,1)} %param.8) | copy-start | bytes 7864324
  91.2 10.9 %slice-start = ((s8[5242880]{0:T(1024)(128)(4,1)}), s8[4194304]{0:T(1024)(128)(4,1)S(1)}, s32[]{:S(2)}) async-start(s8[5242880]{0:T(1024)(128)(4,1)} %bitcast.105), calls=%async_computation | async-start | bytes 8388608
  96.4 5.7 %slice-start.1 = ((s8[5242880]{0:T(1024)(128)(4,1)}), s8[1048576]{0:T(1024)(128)(4,1)S(1)}, s32[]{:S(2)}) async-start(s8[5242880]{0:T(1024)(128)(4,1)} %bitcast.105), calls=%async_computation.1 | async-start | bytes 2097152
  96.4 24.9 %collective-permute-start.5 = (f32[8,128,128]{2,1,0:T(8,128)S(1)}, f32[8,128,128]{2,1,0:T(8,128)S(1)}, u32[]{:S(2)}, u32[]{:S(2)}) collective-permute-start(f32[8,128,128]{2,1,0:T(8,128)S(1)} %bitcast.120), channel_id=1, source_target_pairs={{4,0},{8,4},{12,8},{5,1},{9,5},{13,9},{6,2},{10,6},{14,10},{7,3},{... | collective-permute-start | bytes 1572872 | tf_op jit(solution)/shard_map/ppermute | solution.py:17
  97.8 4.2 %copy-start.8 = (bf16[8,1280,128]{2,1,0:T(8,128)(2,1)S(1)}, bf16[8,1280,128]{2,1,0:T(8,128)(2,1)}, u32[]{:S(2)}) copy-start(bf16[8,1280,128]{2,1,0:T(8,128)(2,1)} %param.7) | copy-start | bytes 7864324
  102.1 21.1 %copy-start.5 = (f32[8,5,128,128]{3,1,2,0:T(8,128)S(1)}, f32[8,5,128,128]{3,1,2,0:T(8,128)}, u32[]{:S(2)}) copy-start(f32[8,5,128,128]{3,1,2,0:T(8,128)} %copy.42) | copy-start | bytes 7864324
  121.4 4.1 %copy-start.4 = (bf16[8,1280,128]{2,1,0:T(8,128)(2,1)S(1)}, bf16[8,1280,128]{2,1,0:T(8,128)(2,1)}, u32[]{:S(2)}) copy-start(bf16[8,1280,128]{2,1,0:T(8,128)(2,1)} %copy-done.3) | copy-start | bytes 7864324
  121.4 4.1 %copy-start.13 = (bf16[8,5,128,128]{3,2,1,0:T(8,128)(2,1)S(1)}, bf16[8,5,128,128]{3,2,1,0:T(8,128)(2,1)}, u32[]{:S(2)}) copy-start(bf16[8,5,128,128]{3,2,1,0:T(8,128)(2,1)} %copy-done.12) | copy-start | bytes 3932164
  121.4 28.5 %collective-permute-start.7 = (f32[8,128,128]{2,1,0:T(8,128)S(1)}, f32[8,128,128]{2,1,0:T(8,128)S(1)}, u32[]{:S(2)}, u32[]{:S(2)}) collective-permute-start(f32[8,128,128]{2,1,0:T(8,128)S(1)} %multiply_add_fusion.1), channel_id=1, source_target_pairs={{8,0},{12,4},{9,1},{13,5},{10,2},{14,6},{11,3},{15,7},{24,16},{28,... | collective-permute-start | bytes 1572872 | tf_op jit(solution)/shard_map/ppermute | solution.py:17
  123.2 27.4 %slice-start.2 = ((s8[5242880]{0:T(1024)(128)(4,1)}), s8[4194304]{0:T(1024)(128)(4,1)S(1)}, s32[]{:S(2)}) async-start(s8[5242880]{0:T(1024)(128)(4,1)} %bitcast.115), calls=%async_computation.2 | async-start | bytes 8388608
  125.5 25.2 %slice-start.3 = ((s8[5242880]{0:T(1024)(128)(4,1)}), s8[1048576]{0:T(1024)(128)(4,1)S(1)}, s32[]{:S(2)}) async-start(s8[5242880]{0:T(1024)(128)(4,1)} %bitcast.115), calls=%async_computation.3 | async-start | bytes 2097152
  150.6 2.4 %copy-start.11 = (bf16[8,1280,128]{2,1,0:T(8,128)(2,1)S(1)}, bf16[8,1280,128]{2,1,0:T(8,128)(2,1)}, u32[]{:S(2)}) copy-start(bf16[8,1280,128]{2,1,0:T(8,128)(2,1)} %param.8) | copy-start | bytes 7864324
